TPU v7x, 32 devices: a whole 2x2x4 slice. The times are simulated.
32 devices in a mesh: groups: 2 (over y), seq: 4 (over z), head: 2 (over x), sub: 2 (over core).
Axes of the slice: x: 2, y: 2, z: 4, core: 2. Of those that a mesh axis runs over, the one named last changes fastest.
Arguments:
- queries: bfloat16 [64, 1024, 128], P(('head', 'sub'), ('groups', 'seq')), parts along dimension 1, may hold values from -6 to 6
- keys_values: bfloat16 [8, 1024, 256], P(('head', 'sub'), ('groups', 'seq')), parts along dimension 1, may hold values from -6 to 6
- student_x: bfloat16 [64, 1024, 128], P(('head', 'sub'), ('groups', 'seq')), parts along dimension 1, may hold values from -32 to 32
- state_maps: bfloat16 [8, 1024, 128], P(('head', 'sub'), ('groups', 'seq')), parts along dimension 1, may hold values from -0.75 to 0.75
- decay_logit: float32 [64, 1024], P(('head', 'sub'), ('groups', 'seq')), parts along dimension 1, may hold values from 0 to 16
- skip_gain: float32 [64], P(('head', 'sub')), may hold values from 0.5 to 2
- init_state: float32 [128, 64, 128], P(('groups', 'head', 'sub')), parts along dimension 0, may hold values from -6 to 6
Outputs:
- grad_x: bfloat16 [64, 1024, 128], P(('head', 'sub'), ('groups', 'seq')), parts along dimension 1
- grad_maps: bfloat16 [8, 1024, 128], P(('head', 'sub'), ('groups', 'seq')), parts along dimension 1
- grad_log_decay: float32 [64, 1024], P(('head', 'sub'), ('groups', 'seq')), parts along dimension 1
There are 2 independent parts, one for each index of `groups`. A program takes and returns all parts, laid end to end along the dimension named above; an argument that names none is the same for every part. Nothing has to cross between parts.
All inputs are finite; a program needn't handle non-finite values.
Results may differ from a plain program's by a relative error of at most 0.013.
Values may be sent and summed in bfloat16 or wider, within the bound.
No kernel may reach another device: no remote copies, remote signals or barrier semaphores. Data moves between devices by JAX's collectives and lax.ppermute only.
A program may use at most 64 MiB of HBM per device.

v0:
```python
import math
import jax
import jax.numpy as jnp
from jax import lax
from jax.sharding import PartitionSpec as P

epsilon = 1e-05
highest = lax.Precision.HIGHEST


def entering_2(x, axis, join, neutral):
    place = lax.axis_index(axis)
    gathered = jax.tree.map(
        lambda a, kind: lax.all_gather(a.astype(kind), axis), x, (jnp.bfloat16, jnp.bfloat16)
    )
    state = jax.tree.map(lambda a, e: jnp.zeros_like(a) + jnp.asarray(e, a.dtype), x, neutral)

    def entering_one(turn, state):
        return join(
            state,
            jax.tree.map(
                lambda a, own: lax.dynamic_index_in_dim(a, turn, 0, False).astype(own.dtype),
                gathered,
                x,
            ),
        )

    return lax.fori_loop(0, place, entering_one, state)


def prefix(x, axis, join, neutral):
    count = lax.axis_size(axis)
    place = lax.axis_index(axis)
    ahead = count - 1 - place
    gathered = jax.tree.map(
        lambda a, kind: lax.all_gather(a.astype(kind), axis),
        x,
        jax.tree.map(lambda a: jnp.bfloat16 if a.dtype == jnp.float32 else a.dtype, x),
    )
    state = jax.tree.map(lambda a, e: jnp.zeros_like(a) + jnp.asarray(e, a.dtype), x, neutral)

    def prefix_one(turn, state):
        source = count - 1 - turn
        return join(
            state,
            jax.tree.map(
                lambda a, own: lax.dynamic_index_in_dim(a, source, 0, False).astype(own.dtype),
                gathered,
                x,
            ),
        )

    return lax.fori_loop(0, ahead, prefix_one, state)


def attend(query_rows, positions, keys_values, tok_dev):
    group_count, row_count, head_width = query_rows.shape
    score_scale = head_width ** (-0.5)
    start_max = jnp.full((group_count, row_count), -1e30, jnp.float32)
    start_sum = jnp.zeros((group_count, row_count), jnp.float32)
    start_acc = jnp.zeros((group_count, row_count, head_width), jnp.float32)
    shards = lax.all_gather(keys_values, "seq", axis=1, tiled=True)
    block_rows = math.gcd(shards.shape[1], tok_dev)

    def one_block(number, running):
        running_max, running_sum, weighted = running
        key_block = lax.dynamic_slice_in_dim(shards, number * block_rows, block_rows, 1)
        scores = (
            jnp.einsum(
                "grd,gkd->grk",
                query_rows,
                key_block[:, :, :head_width],
                preferred_element_type=jnp.float32,
            )
            * score_scale
        )
        key_positions = number * block_rows + jnp.arange(block_rows)
        allowed = (positions[:, None] >= key_positions[None, :])[None]
        scores = jnp.where(allowed, scores, -1e30)
        new_max = jnp.maximum(running_max, jnp.max(scores, axis=2))
        weights = jnp.where(allowed, jnp.exp(scores - new_max[..., None]), 0.0)
        factor = jnp.exp(running_max - new_max)
        running_sum = running_sum * factor + jnp.sum(weights, axis=2)
        weighted = weighted * factor[..., None] + jnp.einsum(
            "grk,gkd->grd",
            weights.astype(jnp.bfloat16),
            key_block[:, :, head_width:],
            preferred_element_type=jnp.float32,
        )
        return (new_max, running_sum, weighted)

    running_max, running_sum, weighted = lax.fori_loop(
        0, shards.shape[1] // block_rows, one_block, (start_max, start_sum, start_acc)
    )
    return (weighted / running_sum[..., None]).astype(jnp.bfloat16)


def forward_chain(earlier, later):
    return (earlier[0] * later[0], later[0][:, None, None] * earlier[1] + later[1])


def backward_chain(earlier, later):
    decay_early, state_early, closing_early, sums_early = earlier
    decay_late, state_late, closing_late, sums_late = later
    return (
        decay_early * decay_late,
        decay_late[:, None, None] * state_early + state_late,
        closing_early + decay_early[:, None, None] * closing_late,
        sums_early + sums_late - jnp.sum(closing_late * state_early, axis=(1, 2)),
    )


def body(queries, keys_values, student_x, state_maps, decay_logit, skip_gain, init_state):
    local_heads, tok_dev, head_width = student_x.shape
    local_groups = state_maps.shape[0]
    per_group = local_heads // local_groups
    state_size = state_maps.shape[2] // 2
    seq_count = lax.axis_size("seq")
    seq_rank = lax.axis_index("seq")
    repeat_count = max(1, seq_count // per_group)
    sub_rows = tok_dev // repeat_count
    per_peer = per_group * repeat_count // seq_count
    sectioned = queries.reshape(local_groups, per_group * repeat_count, sub_rows, head_width)
    arrived = lax.all_to_all(sectioned, "seq", split_axis=1, concat_axis=1, tiled=True)
    slot_ids = jnp.arange(seq_count * per_peer)
    source = slot_ids // per_peer
    member = seq_rank * per_peer + slot_ids % per_peer
    starts = source * tok_dev + member % repeat_count * sub_rows
    positions = (starts[:, None] + jnp.arange(sub_rows)[None, :]).reshape(-1)
    answers = attend(arrived.reshape(local_groups, -1, head_width), positions, keys_values, tok_dev)
    answers = answers.reshape(local_groups, seq_count * per_peer, sub_rows, head_width)
    teacher = lax.all_to_all(answers, "seq", split_axis=1, concat_axis=1, tiled=True).reshape(
        local_heads, tok_dev, head_width
    )
    teacher_wide = teacher.astype(jnp.float32)
    target = teacher_wide * lax.rsqrt(
        jnp.mean(teacher_wide * teacher_wide, axis=2, keepdims=True) + epsilon
    )
    log_decay = jax.nn.log_sigmoid(decay_logit)
    cumulative = jnp.cumsum(log_decay, axis=1)
    totals = cumulative[:, -1]
    decays = jnp.exp(totals)
    to_end = jnp.exp(totals[:, None] - cumulative)
    from_start = jnp.exp(cumulative)
    in_maps = state_maps[:, :, :state_size]
    out_maps = state_maps[:, :, state_size:]
    intersection = jnp.einsum("gtn,gsn->gts", out_maps, in_maps, preferred_element_type=jnp.float32)
    order_ids = jnp.arange(tok_dev)
    causal = (order_ids[:, None] >= order_ids[None, :])[None]
    gaps = cumulative[:, :, None] - cumulative[:, None, :]
    decayed = jnp.where(causal, jnp.exp(jnp.where(causal, gaps, 0.0)), 0.0)
    mixing = (
        decayed.reshape(local_groups, per_group, tok_dev, tok_dev) * intersection[:, None]
    ).reshape(local_heads, tok_dev, tok_dev)
    inputs_wide = student_x.astype(jnp.float32)
    in_heads = jnp.repeat(in_maps.astype(jnp.float32), per_group, axis=0)
    out_heads = jnp.repeat(out_maps.astype(jnp.float32), per_group, axis=0)
    local_out = jnp.einsum("hts,hsp->htp", mixing, inputs_wide, precision=highest)
    weighted_in = in_heads * to_end[..., None]
    end_state = jnp.einsum("hsn,hsp->hnp", weighted_in, inputs_wide, precision=highest)
    prefix_decay, prefix_state = entering_2(
        (decays, end_state),
        "seq",
        forward_chain,
        (jnp.ones_like(decays), jnp.zeros_like(end_state)),
    )
    entering = prefix_state + prefix_decay[:, None, None] * init_state
    state_out = local_out + from_start[..., None] * jnp.einsum(
        "htn,hnp->htp", out_heads, entering, precision=highest
    )
    outputs = state_out + skip_gain[:, None, None] * inputs_wide
    inverse = lax.rsqrt(jnp.mean(outputs * outputs, axis=2, keepdims=True) + epsilon)
    normed = outputs * inverse
    residual = normed - target
    grad_out = (residual - normed * jnp.mean(residual * normed, axis=2, keepdims=True)) * inverse
    local_dx = jnp.einsum("hts,htp->hsp", mixing, grad_out, precision=highest)
    cross = jnp.einsum("htp,hsp->hts", grad_out, inputs_wide, precision=highest)
    paired = decayed * cross
    local_din = jnp.einsum("hts,htn->hsn", paired, out_heads, precision=highest)
    grad_output_maps = jnp.einsum("hts,hsn->htn", paired, in_heads, precision=highest)
    grad_output_maps = grad_output_maps + from_start[..., None] * jnp.einsum(
        "hnp,htp->htn", entering, grad_out, precision=highest
    )
    forward_term = jnp.sum(grad_out * state_out, axis=2)
    flow = jnp.einsum(
        "htn,htp->hnp", out_heads * from_start[..., None], grad_out, precision=highest
    )
    closing = jnp.sum(forward_term - jnp.sum(inputs_wide * local_dx, axis=2), axis=1)
    identity = (
        jnp.ones_like(decays),
        jnp.zeros_like(flow),
        jnp.zeros_like(end_state),
        jnp.zeros_like(closing),
    )
    unused_decay, incoming, unused_state, later_sum = prefix(
        (decays, flow, end_state, closing), "seq", backward_chain, identity
    )
    state_dx = local_dx + jnp.einsum("hsn,hnp->hsp", weighted_in, incoming, precision=highest)
    terms = forward_term - jnp.sum(inputs_wide * state_dx, axis=2)
    grad_log_decay = later_sum[:, None] + lax.cumsum(terms, axis=1, reverse=True)
    grad_input_maps = (
        local_din
        + jnp.einsum("hnp,hsp->hsn", incoming, inputs_wide, precision=highest) * to_end[..., None]
    )
    grad_maps = jnp.concatenate([grad_input_maps, grad_output_maps], axis=2)
    grad_maps = grad_maps.reshape(local_groups, per_group, tok_dev, 2 * state_size).sum(axis=1)
    grad_x = state_dx + skip_gain[:, None, None] * grad_out
    return (grad_x.astype(jnp.bfloat16), grad_maps.astype(jnp.bfloat16), grad_log_decay)


def solution(mesh):
    in_specs = (
        P(("head", "sub"), ("groups", "seq"), None),
        P(("head", "sub"), ("groups", "seq"), None),
        P(("head", "sub"), ("groups", "seq"), None),
        P(("head", "sub"), ("groups", "seq"), None),
        P(("head", "sub"), ("groups", "seq")),
        P(("head", "sub")),
        P(("groups", "head", "sub"), None, None),
    )
    out_specs = (
        P(("head", "sub"), ("groups", "seq"), None),
        P(("head", "sub"), ("groups", "seq"), None),
        P(("head", "sub"), ("groups", "seq")),
    )
    return jax.shard_map(body, mesh=mesh, in_specs=in_specs, out_specs=out_specs, check_vma=False)
```

profile of v0, /device:TPU:0, one launch (start us, length us, event | category | flops | bytes accessed | tf_op | source)
XLA Modules:
  0.0 146.4 jit_solution(11512429082375482874)
XLA Ops:
  10.9 6.3 %all-to-all-start = ((bf16[2,8,128,128]{3,2,0,1:T(8,128)(2,1)}), bf16[2,8,128,128]{3,2,0,1:T(8,128)(2,1)S(1)}, u32[]{:S(2)}, u32[]{:S(2)}) async-start(bf16[2,8,128,128]{3,2,0,1:T(8,128)(2,1)} %copy.89), calls=%async_computation | async-start | bytes 1048576 | tf_op jit(solution)/shard_map/all_to_all | solution.py:124
  19.9 18.1 %all-reduce = bf16[64]{0:T(256)(128)(2,1)S(1)} all-reduce(bf16[64]{0:T(256)(128)(2,1)S(1)} %dynamic-update-slice), channel_id=2, replica_groups=mesh['groups'=2,'seq'=4,'head'=2,'sub'=2] {'seq'}, use_global_device_ids=true, to_apply=%add | all-reduce | flops 64 | bytes 256
  39.3 23.4 %all_gather.30 = bf16[2,512,256]{2,1,0:T(8,128)(2,1)} all-gather(bf16[2,128,256]{2,1,0:T(8,128)(2,1)S(1)} %copy-done.17), channel_id=1, replica_groups=mesh['groups'=2,'seq'=4,'head'=2,'sub'=2] {'seq'}, dimensions={1}, use_global_device_ids=true | all-gather | bytes 655360 | tf_op jit(solution)/shard_map/all_gather | solution.py:62
  62.8 2.2 %fusion.49 = f32[16,128,128]{1,2,0:T(8,128)} fusion(f32[16,128,128]{2,1,0:T(8,128)S(1)} %bitcast_multiply_fusion.1, bf16[16,128,128]{2,1,0:T(8,128)(2,1)S(1)} %copy-done), kind=kOutput, calls=%fused_computation.102 | convolution fusion | flops 402653184 | bytes 2621440 | tf_op jit(solution)/shard_map/hts,hsp->htp/dot_general | solution.py:158
  65.0 13.6 %while.49 = (s32[]{:T(128)}, f32[2,1024]{1,0:T(2,128)S(1)}, f32[2,1024]{1,0:T(2,128)S(1)}, f32[2,1024,128]{2,1,0:T(8,128)S(1)}, bf16[2,512,256]{2,1,0:T(8,128)(2...) while((s32[]{:T(128)}, f32[2,1024]{1,0:T(2,128)S(1)}, ...), condition=%wide.region_7.8_spmd.clone, body=%wide.region_4.7_spmd.clone.sunk | while | flops 137505920 | bytes 6563051 | solution.py:92
  66.8 1.6 %convolution_add_fusion.5 = f32[2,1024,128]{2,1,0:T(8,128)S(1)} fusion(f32[2,1024,128]{2,1,0:T(8,128)S(1)} %get-tuple-element.598, f32[2,1024,128]{1,2,0:T(8,128)S(1)} %get-tuple-element.553, f32[2,1024]{1,0:T(2,128)S(1)} %get-tuple-element.555, f32[2,1024]{1,0:T(2,128)S(1)} %fusion.87, pred[]{:T(512)S(6)} %compare.10, ...), kind=kOutput, calls=%fused_computation.14.clone.1 | convolution fusion | flops 68681728 | bytes 3358729 | tf_op jit(solution)/shard_map/while/body/eval_jaxpr/grk,gkd->grd/dot_general | solution.py:84
  70.2 1.6 %convolution_add_fusion.5 = f32[2,1024,128]{2,1,0:T(8,128)S(1)} fusion(f32[2,1024,128]{2,1,0:T(8,128)S(1)} %get-tuple-element.598, f32[2,1024,128]{1,2,0:T(8,128)S(1)} %get-tuple-element.553, f32[2,1024]{1,0:T(2,128)S(1)} %get-tuple-element.555, f32[2,1024]{1,0:T(2,128)S(1)} %fusion.87, pred[]{:T(512)S(6)} %compare.10, ...), kind=kOutput, calls=%fused_computation.14.clone.1 | convolution fusion | flops 68681728 | bytes 3358729 | tf_op jit(solution)/shard_map/while/body/eval_jaxpr/grk,gkd->grd/dot_general | solution.py:84
  73.6 1.6 %convolution_add_fusion.5 = f32[2,1024,128]{2,1,0:T(8,128)S(1)} fusion(f32[2,1024,128]{2,1,0:T(8,128)S(1)} %get-tuple-element.598, f32[2,1024,128]{1,2,0:T(8,128)S(1)} %get-tuple-element.553, f32[2,1024]{1,0:T(2,128)S(1)} %get-tuple-element.555, f32[2,1024]{1,0:T(2,128)S(1)} %fusion.87, pred[]{:T(512)S(6)} %compare.10, ...), kind=kOutput, calls=%fused_computation.14.clone.1 | convolution fusion | flops 68681728 | bytes 3358729 | tf_op jit(solution)/shard_map/while/body/eval_jaxpr/grk,gkd->grd/dot_general | solution.py:84
  77.0 1.6 %convolution_add_fusion.5 = f32[2,1024,128]{2,1,0:T(8,128)S(1)} fusion(f32[2,1024,128]{2,1,0:T(8,128)S(1)} %get-tuple-element.598, f32[2,1024,128]{1,2,0:T(8,128)S(1)} %get-tuple-element.553, f32[2,1024]{1,0:T(2,128)S(1)} %get-tuple-element.555, f32[2,1024]{1,0:T(2,128)S(1)} %fusion.87, pred[]{:T(512)S(6)} %compare.10, ...), kind=kOutput, calls=%fused_computation.14.clone.1 | convolution fusion | flops 68681728 | bytes 3358729 | tf_op jit(solution)/shard_map/while/body/eval_jaxpr/grk,gkd->grd/dot_general | solution.py:84
  80.0 3.5 %all-to-all-start.1 = ((bf16[2,8,128,128]{2,3,0,1:T(8,128)(2,1)}), bf16[2,8,128,128]{2,3,0,1:T(8,128)(2,1)S(1)}, u32[]{:S(2)}, u32[]{:S(2)}) async-start(bf16[2,8,128,128]{2,3,0,1:T(8,128)(2,1)} %copy.91), calls=%async_computation.1 | async-start | bytes 1048576 | tf_op jit(solution)/shard_map/all_to_all | solution.py:132
  85.1 3.3 %multiply_reduce_fusion.3 = (f32[16,128]{1,0:T(8,128)S(1)}, f32[16,128,128]{1,2,0:T(8,128)S(1)}) fusion(bf16[16,128,128]{1,2,0:T(8,128)(2,1)S(1)} %copy.88, f32[16]{0:T(128)S(1)} %copy-done.18, f32[16,128,128]{1,2,0:T(8,128)} %fusion.49, f32[16,128,64]{1,2,0:T(8,128)S(1)} %bitcast.93, f32[16,64,128]{2,1,0:T(8,128)S(1)} %get-tuple-element.293, ...), kind=kOutput, calls=%fused_computation.67 | convolution fusion | flops 203421696 | bytes 4210816 | tf_op jit(solution)/shard_map/htn,hnp->htp/dot_general | solution.py:168
  88.4 5.4 %all-to-all-done.1 = bf16[2,8,128,128]{2,3,0,1:T(8,128)(2,1)S(1)} async-done(((bf16[2,8,128,128]{2,3,0,1:T(8,128)(2,1)}), bf16[2,8,128,128]{2,3,0,1:T(8,128)(2,1)S(1)}, u32[]{:S(2)}, u32[]{:S(2)}) %all-to-all-start.1) | async-done | bytes 524320 | tf_op jit(solution)/shard_map/all_to_all | solution.py:132
  95.5 2.8 %convolution_convert_fusion = bf16[16,64,128]{2,1,0:T(8,128)(2,1)} fusion(f32[16,128,128]{1,2,0:T(8,128)S(1)} %get-tuple-element.394, f32[16,128,64]{1,2,0:T(8,128)S(1)} %bitcast.94, f32[16,128]{1,0:T(8,128)S(1)} %get-tuple-element.404), kind=kOutput, calls=%fused_computation.51 | convolution fusion | flops 201588736 | bytes 1843200 | tf_op jit(solution)/shard_map/htn,htp->hnp/dot_general | solution.py:185
  98.3 2.2 %fusion.28 = (f32[16,128]{1,0:T(8,128)S(1)}, f32[16,128,128]{1,2,0:T(8,128)}) fusion(bf16[16,128,128]{1,2,0:T(8,128)(2,1)S(1)} %copy.88, f32[16,128,128]{2,1,0:T(8,128)S(1)} %copy-done.3, f32[16,128,128]{1,2,0:T(8,128)S(1)} %get-tuple-element.394), kind=kOutput, calls=%fused_computation.54 | convolution fusion | flops 403437568 | bytes 3678208 | tf_op jit(solution)/shard_map/hts,htp->hsp/dot_general | solution.py:176
  100.9 10.3 %all-reduce.1 = bf16[64]{0:T(256)(128)(2,1)S(1)} all-reduce(bf16[64]{0:T(256)(128)(2,1)S(1)} %dynamic-update-slice.1), channel_id=5, replica_groups=mesh['groups'=2,'seq'=4,'head'=2,'sub'=2] {'seq'}, use_global_device_ids=true, to_apply=%add.1 | all-reduce | flops 64 | bytes 256
  111.2 2.2 %convolution_multiply_fusion.3 = f32[16,128,64]{1,2,0:T(8,128)S(1)} fusion(f32[16,128,128]{1,2,0:T(8,128)S(1)} %get-tuple-element.394, f32[16,128]{1,0:T(8,128)S(1)} %get-tuple-element.404, f32[16,64,128]{2,1,0:T(8,128)S(1)} %get-tuple-element.293, f32[16,64,128]{2,1,0:T(8,128)} %param.19, f32[16]{0:T(128)S(1)} %get-tuple-element.294), kind=kOutput, calls=%fused_computation.46 | convolution fusion | flops 201719808 | bytes 2629696 | tf_op jit(solution)/shard_map/hnp,htp->htn/dot_general | solution.py:181
  115.7 2.9 %convolution_add_fusion.2 = f32[16,128,64]{1,2,0:T(8,128)} fusion(f32[16,128,64]{1,2,0:T(8,128)S(1)} %convolution_multiply_fusion.3, f32[16,128,128]{2,1,0:T(8,128)S(1)} %convolution_multiply_fusion.1, f32[16,128,64]{1,2,0:T(8,128)S(1)} %bitcast.97), kind=kOutput, calls=%fused_computation.47 | convolution fusion | flops 201457664 | bytes 2621440 | tf_op jit(solution)/shard_map/hts,hsn->htn/dot_general | solution.py:180
  118.6 7.5 %all-gather.9.cloned.1.call-done = bf16[64,64,128]{2,1,0:T(8,128)(2,1)} async-done(((bf16[16,64,128]{2,1,0:T(8,128)(2,1)}), bf16[64,64,128]{2,1,0:T(8,128)(2,1)}) %all-gather.9.cloned.1.call-update) | async-done | bytes 1048592 | tf_op jit(solution)/shard_map/all_gather | solution.py:36
  126.1 4.4 %while.48 = (s32[]{:T(128)}, f32[16,64,128]{2,1,0:T(8,128)S(1)}, f32[16]{0:T(128)S(1)}, s32[]{:T(128)}, bf16[4,16]{1,0:T(4,128)(2,1)S(1)}, /*index=5*/bf16[4,16,...) while((s32[]{:T(128)}, f32[16,64,128]{2,1,0:T(8,128)S(1)}, ...), condition=%wide.region_15.16_spmd, body=%wide.region_13.15_spmd.sunk | while | flops 786486 | bytes 1573487 | solution.py:53
  126.2 1.3 fusion.81
  127.5 1.3 fusion.81
  128.9 1.3 fusion.81
  131.7 2.8 %fusion.29 = (f32[16,128]{1,0:T(8,128)S(1)}, bf16[16,128,128]{1,2,0:T(8,128)(2,1)}) fusion(bf16[16,128,128]{1,2,0:T(8,128)(2,1)S(1)} %copy.88, f32[16,128,128]{1,2,0:T(8,128)S(1)} %get-tuple-element.394, f32[16]{0:T(128)S(1)} %copy-done.18, f32[16,128,128]{1,2,0:T(8,128)S(1)} %copy-done.11, f32[16,64,128]{2,1,0:T(8,128)S(1)} %get-tuple-element.297, ...), kind=kOutput, calls=%fused_computation.55 | convolution fusion | flops 203290624 | bytes 4210752 | tf_op jit(solution)/shard_map/hsn,hnp->hsp/dot_general | solution.py:198
  137.6 1.2 reduce_window_sum.22
  (135 shorter events, 26.1 us)
Async XLA Ops:
  7.2 1.4 copy-start.15
  7.2 1.7 %copy-start = (bf16[16,128,128]{2,1,0:T(8,128)(2,1)S(1)}, bf16[16,128,128]{2,1,0:T(8,128)(2,1)}, u32[]{:S(2)}) copy-start(bf16[16,128,128]{2,1,0:T(8,128)(2,1)} %param.15) | copy-start | bytes 1572868
  7.2 76.4 %all-gather.7.cloned.1.call-start = ((), (), s32[]{:S(2)}) async-start(), calls=%async_computation.2 | async-start | bytes 1310720 | tf_op jit(solution)/shard_map/all_gather | solution.py:14
  8.8 1.3 copy-start.9
  8.8 1.3 copy-start.16
  10.9 54.0 %all-to-all-start = ((bf16[2,8,128,128]{3,2,0,1:T(8,128)(2,1)}), bf16[2,8,128,128]{3,2,0,1:T(8,128)(2,1)S(1)}, u32[]{:S(2)}, u32[]{:S(2)}) async-start(bf16[2,8,128,128]{3,2,0,1:T(8,128)(2,1)} %copy.89), calls=%async_computation | async-start | bytes 1048576 | tf_op jit(solution)/shard_map/all_to_all | solution.py:124
  17.8 0.7 copy-start.19
  38.4 0.9 copy-start.17
  38.8 24.0 %copy-start.2 = (f32[16,128,128]{2,1,0:T(8,128)}, f32[16,128,128]{2,1,0:T(8,128)S(1)}, u32[]{:S(2)}) copy-start(f32[16,128,128]{2,1,0:T(8,128)S(1)} %bitcast_multiply_fusion.1) | copy-start | bytes 3145732
  80.0 13.7 %all-to-all-start.1 = ((bf16[2,8,128,128]{2,3,0,1:T(8,128)(2,1)}), bf16[2,8,128,128]{2,3,0,1:T(8,128)(2,1)S(1)}, u32[]{:S(2)}, u32[]{:S(2)}) async-start(bf16[2,8,128,128]{2,3,0,1:T(8,128)(2,1)} %copy.91), calls=%async_computation.1 | async-start | bytes 1048576 | tf_op jit(solution)/shard_map/all_to_all | solution.py:132
  83.5 42.5 %all-gather.9.cloned.1.call-start = ((), (), s32[]{:S(2)}) async-start(), calls=%async_computation.3 | async-start | bytes 1310720 | tf_op jit(solution)/shard_map/all_gather | solution.py:36
  83.8 1.2 copy-start.14
  83.9 4.4 %copy-start.6 = (f32[2,8,128,64]{2,3,1,0:T(8,128)}, f32[2,8,128,64]{2,3,1,0:T(8,128)S(1)}, u32[]{:S(2)}) copy-start(f32[2,8,128,64]{2,3,1,0:T(8,128)S(1)} %broadcast_in_dim.109) | copy-start | bytes 1572868
  83.9 1.2 copy-start.18
  94.4 1.0 copy-start.7
  95.5 2.9 %copy-start.3 = (f32[16,128,128]{2,1,0:T(8,128)S(1)}, f32[16,128,128]{2,1,0:T(8,128)}, u32[]{:S(2)}) copy-start(f32[16,128,128]{2,1,0:T(8,128)} %copy-done.2) | copy-start | bytes 3145732
  111.2 2.2 %copy-start.1 = (bf16[16,128,128]{2,1,0:T(8,128)(2,1)S(1)}, bf16[16,128,128]{2,1,0:T(8,128)(2,1)}, u32[]{:S(2)}) copy-start(bf16[16,128,128]{2,1,0:T(8,128)(2,1)} %param.15) | copy-start | bytes 1572868
  113.4 2.2 %copy-start.10 = (f32[2,8,128,64]{2,3,1,0:T(8,128)S(1)}, f32[2,8,128,64]{2,3,1,0:T(8,128)}, u32[]{:S(2)}) copy-start(f32[2,8,128,64]{2,3,1,0:T(8,128)} %copy-done.9) | copy-start | bytes 1572868
  114.7 1.0 copy-start.4
  130.5 1.2 copy-start.11
  131.7 2.8 %copy-start.5 = (f32[16,128,128]{2,1,0:T(8,128)S(1)}, f32[16,128,128]{2,1,0:T(8,128)}, u32[]{:S(2)}) copy-start(f32[16,128,128]{2,1,0:T(8,128)} %copy-done.4) | copy-start | bytes 3145732
  131.7 2.8 %copy-start.8 = (f32[2,8,128,64]{2,3,1,0:T(8,128)S(1)}, f32[2,8,128,64]{2,3,1,0:T(8,128)}, u32[]{:S(2)}) copy-start(f32[2,8,128,64]{2,3,1,0:T(8,128)} %copy-done.6) | copy-start | bytes 1572868
  134.5 1.1 copy-start.12
  135.6 1.0 copy-start.13
Sparse Core Ops, SparseCore 0:
  10.2 41.8 all-gather.6
  98.5 27.5 all-gather.8
where the time goes:
time: 147 us; the launch traced here: 146 us
  blocking collectives  51.8 us (35%)
  matrix products  34.5 us (23%)
  between operations  15.2 us (10%)
  waiting for transfers between devices  12.9 us (9%)
  other arithmetic  11.2 us (8%)
  local copies, waits for them, and re-layouts  10.1 us (7%)
  starting transfers between devices  9.87 us (7%)
    unnamed x2, blocking collectives  28.3 us
    all_gather x1, blocking collectives, attend(): shards = lax.all_gather(keys_values, 'seq', axis=1, tiled=True)  23.4 us
    unnamed x51, local copies, waits for them, and re-layouts  7.57 us
    all_gather x1, waiting for transfers between devices, prefix(): lax.all_gather(a.astype(kind), axis)  7.49 us
    dot_general x4, matrix products, one_block(): jnp.einsum('grk,gkd->grd', weights.astype(jnp.bfloat16), key_block[:, :,...  6.51 us
    all_to_all x1, starting transfers between devices, body(): lax.all_to_all(sectioned, 'seq', split_axis=1, concat_axis=1, tiled=True)  6.32 us
    all_to_all x1, waiting for transfers between devices, body(): lax.all_to_all(answers, 'seq', split_axis=1, concat_axis=1, tiled=True)  5.39 us
    dot_general x4, matrix products, one_block(): jnp.einsum('grd,gkd->grk', query_rows, key_block[:, :, :head_width], pref...  4.86 us
  transfers between devices with their start and end apart: 4, of which 2 were waited for; matrix products, arithmetic and copies ran while one was open for 22% of the time, Pallas kernels for 0%

commit v1 on v0

--- a/solution.py
+++ b/solution.py
@@ -6,6 +6,18 @@
 
 epsilon = 1e-05
 highest = lax.Precision.HIGHEST
+
+
+def split_up(x, dim, peers):
+    lengths = x.shape
+    pieces = x.reshape(*lengths[:dim], peers, lengths[dim] // peers, *lengths[dim + 1 :])
+    return jnp.moveaxis(pieces, dim, 0)
+
+
+def in_order(pieces, dim):
+    shape = list(pieces.shape[1:])
+    shape[dim] *= pieces.shape[0]
+    return jnp.moveaxis(pieces, 0, dim).reshape(shape)
 
 
 def entering_2(x, axis, join, neutral):
@@ -121,7 +133,14 @@
     sub_rows = tok_dev // repeat_count
     per_peer = per_group * repeat_count // seq_count
     sectioned = queries.reshape(local_groups, per_group * repeat_count, sub_rows, head_width)
-    arrived = lax.all_to_all(sectioned, "seq", split_axis=1, concat_axis=1, tiled=True)
+    size, index = (lax.axis_size("seq"), lax.axis_index("seq"))
+    tiles = split_up(sectioned, 1, size)
+    finished = [tiles[index]]
+    for lap in range(1, size):
+        sent = tiles[(index + lap) % size]
+        finished.append(lax.ppermute(sent, "seq", [(i, (i + lap) % size) for i in range(size)]))
+    tiles = jnp.stack(finished)[(index - jnp.arange(size)) % size]
+    arrived = in_order(tiles, 1)
     slot_ids = jnp.arange(seq_count * per_peer)
     source = slot_ids // per_peer
     member = seq_rank * per_peer + slot_ids % per_peer

time: 147 us -> 143 us (0.973)
  waiting for transfers between devices: 12.9 us -> 6.24 us
  blocking collectives: 51.8 us -> 48.2 us
  local copies, waits for them, and re-layouts: 10.1 us -> 12.7 us
    ppermute x0 -> x3, starting transfers between devices: none -> 7.01 us  [body(): lax.ppermute(sent, 'seq', [(i, (i + lap) % size) for i in range(size)])]
    all_to_all x1 -> x0, starting transfers between devices: 6.32 us -> none  [body(): lax.all_to_all(sectioned, 'seq', split_axis=1, concat_axis=1, tiled=True)]
    all_to_all x1, waiting for transfers between devices: 5.39 us -> 0.01 us  [body(): lax.all_to_all(answers, 'seq', split_axis=1, concat_axis=1, tiled=True)]
    unnamed x2, blocking collectives: 28.3 us -> 24.5 us
    unnamed x51 -> x45, local copies, waits for them, and re-layouts: 7.57 us -> 9.21 us
  transfers between devices with their start and end apart: 4 -> 6, of which waited for: 2 -> 1; matrix products, arithmetic and copies ran while one was open for 22% -> 23% of each run, Pallas kernels for 0% -> 0%
where the time goes in v1:
time: 143 us; the launch traced here: 142 us
  blocking collectives  48.2 us (34%)
  matrix products  35.7 us (25%)
  between operations  15.1 us (11%)
  local copies, waits for them, and re-layouts  12.7 us (9%)
  other arithmetic  11.8 us (8%)
  starting transfers between devices  11.3 us (8%)
  waiting for transfers between devices  6.24 us (4%)
    unnamed x2, blocking collectives  24.5 us
    all_gather x1, blocking collectives, attend(): shards = lax.all_gather(keys_values, 'seq', axis=1, tiled=True)  23.7 us
    unnamed x45, local copies, waits for them, and re-layouts  9.21 us
    ppermute x3, starting transfers between devices, body(): lax.ppermute(sent, 'seq', [(i, (i + lap) % size) for i in range(size)])  7.01 us
    dot_general x4, matrix products, one_block(): jnp.einsum('grk,gkd->grd', weights.astype(jnp.bfloat16), key_block[:, :,...  6.51 us
    all_gather x1, waiting for transfers between devices, prefix(): lax.all_gather(a.astype(kind), axis)  6.18 us
    dot_general x4, matrix products, one_block(): jnp.einsum('grd,gkd->grk', query_rows, key_block[:, :, :head_width], pref...  4.86 us
    all_to_all x1, starting transfers between devices, body(): lax.all_to_all(answers, 'seq', split_axis=1, concat_axis=1, tiled=True)  4.27 us
  transfers between devices with their start and end apart: 6, of which 1 were waited for; matrix products, arithmetic and copies ran while one was open for 23% of the time, Pallas kernels for 0%

profile of v1, /device:TPU:0, one launch (start us, length us, event | category | flops | bytes accessed | tf_op | source)
XLA Modules:
  0.0 142.0 jit_solution(13874631146100308465)
XLA Ops:
  8.5 3.1 %collective-permute-start = (bf16[2,2,128,128]{3,2,1,0:T(8,128)(2,1)S(1)}, bf16[2,2,128,128]{3,2,1,0:T(8,128)(2,1)S(1)}, u32[]{:S(2)}, u32[]{:S(2)}) collective-permute-start(bf16[2,2,128,128]{3,2,1,0:T(8,128)(2,1)S(1)} %get-tuple-element.406), channel_id=1, source_target_pairs={{0,4},{4,8},{8,12},{12,0},{1,5},{5,9},{9,13},{13,1},{2,6},{6,10},{... | collective-permute-start | bytes 393224 | tf_op jit(solution)/shard_map/ppermute | solution.py:141
  11.5 2.6 %collective-permute-start.1 = (bf16[2,2,128,128]{3,2,1,0:T(8,128)(2,1)S(1)}, bf16[2,2,128,128]{3,2,1,0:T(8,128)(2,1)S(1)}, u32[]{:S(2)}, u32[]{:S(2)}) collective-permute-start(bf16[2,2,128,128]{3,2,1,0:T(8,128)(2,1)S(1)} %get-tuple-element.405), channel_id=1, source_target_pairs={{0,8},{4,12},{8,0},{12,4},{1,9},{5,13},{9,1},{13,5},{2,10},{6,14},... | collective-permute-start | bytes 393224 | tf_op jit(solution)/shard_map/ppermute | solution.py:141
  14.1 1.3 collective-permute-start.2
  19.3 23.7 %all_gather.30 = bf16[2,512,256]{2,1,0:T(8,128)(2,1)} all-gather(bf16[2,128,256]{2,1,0:T(8,128)(2,1)S(1)} %copy-done.13), channel_id=1, replica_groups=mesh['groups'=2,'seq'=4,'head'=2,'sub'=2] {'seq'}, dimensions={1}, use_global_device_ids=true | all-gather | bytes 655360 | tf_op jit(solution)/shard_map/all_gather | solution.py:74
  43.8 13.6 %while.49 = (s32[]{:T(128)}, f32[2,1024]{1,0:T(2,128)S(1)}, f32[2,1024]{1,0:T(2,128)S(1)}, f32[2,1024,128]{2,1,0:T(8,128)S(1)}, bf16[2,512,256]{2,1,0:T(8,128)(2...) while((s32[]{:T(128)}, f32[2,1024]{1,0:T(2,128)S(1)}, ...), condition=%wide.region_7.8_spmd.clone, body=%wide.region_4.7_spmd.clone.sunk | while | flops 137505920 | bytes 6563051 | solution.py:104
  45.5 1.6 %convolution_add_fusion.5 = f32[2,1024,128]{2,1,0:T(8,128)S(1)} fusion(f32[2,1024,128]{2,1,0:T(8,128)S(1)} %get-tuple-element.605, f32[2,1024,128]{1,2,0:T(8,128)S(1)} %get-tuple-element.560, f32[2,1024]{1,0:T(2,128)S(1)} %get-tuple-element.562, f32[2,1024]{1,0:T(2,128)S(1)} %fusion.89, pred[]{:T(512)S(6)} %compare.20, ...), kind=kOutput, calls=%fused_computation.15.clone.1 | convolution fusion | flops 68681728 | bytes 3358729 | tf_op jit(solution)/shard_map/while/body/eval_jaxpr/grk,gkd->grd/dot_general | solution.py:96
  48.9 1.6 %convolution_add_fusion.5 = f32[2,1024,128]{2,1,0:T(8,128)S(1)} fusion(f32[2,1024,128]{2,1,0:T(8,128)S(1)} %get-tuple-element.605, f32[2,1024,128]{1,2,0:T(8,128)S(1)} %get-tuple-element.560, f32[2,1024]{1,0:T(2,128)S(1)} %get-tuple-element.562, f32[2,1024]{1,0:T(2,128)S(1)} %fusion.89, pred[]{:T(512)S(6)} %compare.20, ...), kind=kOutput, calls=%fused_computation.15.clone.1 | convolution fusion | flops 68681728 | bytes 3358729 | tf_op jit(solution)/shard_map/while/body/eval_jaxpr/grk,gkd->grd/dot_general | solution.py:96
  52.3 1.6 %convolution_add_fusion.5 = f32[2,1024,128]{2,1,0:T(8,128)S(1)} fusion(f32[2,1024,128]{2,1,0:T(8,128)S(1)} %get-tuple-element.605, f32[2,1024,128]{1,2,0:T(8,128)S(1)} %get-tuple-element.560, f32[2,1024]{1,0:T(2,128)S(1)} %get-tuple-element.562, f32[2,1024]{1,0:T(2,128)S(1)} %fusion.89, pred[]{:T(512)S(6)} %compare.20, ...), kind=kOutput, calls=%fused_computation.15.clone.1 | convolution fusion | flops 68681728 | bytes 3358729 | tf_op jit(solution)/shard_map/while/body/eval_jaxpr/grk,gkd->grd/dot_general | solution.py:96
  55.8 1.6 %convolution_add_fusion.5 = f32[2,1024,128]{2,1,0:T(8,128)S(1)} fusion(f32[2,1024,128]{2,1,0:T(8,128)S(1)} %get-tuple-element.605, f32[2,1024,128]{1,2,0:T(8,128)S(1)} %get-tuple-element.560, f32[2,1024]{1,0:T(2,128)S(1)} %get-tuple-element.562, f32[2,1024]{1,0:T(2,128)S(1)} %fusion.89, pred[]{:T(512)S(6)} %compare.20, ...), kind=kOutput, calls=%fused_computation.15.clone.1 | convolution fusion | flops 68681728 | bytes 3358729 | tf_op jit(solution)/shard_map/while/body/eval_jaxpr/grk,gkd->grd/dot_general | solution.py:96
  58.8 4.3 %all-to-all-start = ((bf16[2,8,128,128]{2,3,0,1:T(8,128)(2,1)}), bf16[2,8,128,128]{2,3,0,1:T(8,128)(2,1)S(1)}, u32[]{:S(2)}, u32[]{:S(2)}) async-start(bf16[2,8,128,128]{2,3,0,1:T(8,128)(2,1)} %copy.127), calls=%async_computation | async-start | bytes 1048576 | tf_op jit(solution)/shard_map/all_to_all | solution.py:151
  65.6 12.2 %all-reduce = bf16[64]{0:T(256)(128)(2,1)S(1)} all-reduce(bf16[64]{0:T(256)(128)(2,1)S(1)} %dynamic-update-slice), channel_id=2, replica_groups=mesh['groups'=2,'seq'=4,'head'=2,'sub'=2] {'seq'}, use_global_device_ids=true, to_apply=%add | all-reduce | flops 64 | bytes 256
  79.6 2.2 %fusion.51 = f32[16,128,128]{1,2,0:T(8,128)} fusion(f32[16,128,128]{2,1,0:T(8,128)S(1)} %bitcast_multiply_fusion.1, bf16[16,128,128]{2,1,0:T(8,128)(2,1)S(1)} %copy-done), kind=kOutput, calls=%fused_computation.115 | convolution fusion | flops 402653184 | bytes 2621440 | tf_op jit(solution)/shard_map/hts,hsp->htp/dot_general | solution.py:177
  83.4 3.3 %multiply_reduce_fusion.3 = (f32[16,128]{1,0:T(8,128)S(1)}, f32[16,128,128]{1,2,0:T(8,128)S(1)}) fusion(bf16[16,128,128]{1,2,0:T(8,128)(2,1)S(1)} %copy.121, f32[16]{0:T(128)S(1)} %copy-done.15, f32[16,128,128]{1,2,0:T(8,128)} %fusion.51, f32[16,128,64]{1,2,0:T(8,128)S(1)} %bitcast.115, f32[16,64,128]{2,1,0:T(8,128)S(1)} %get-tuple-element.293, ...), kind=kOutput, calls=%fused_computation.68 | convolution fusion | flops 203421696 | bytes 4210816 | tf_op jit(solution)/shard_map/htn,hnp->htp/dot_general | solution.py:187
  87.2 1.8 %multiply_reduce_fusion = (f32[16,128]{1,0:T(8,128)S(1)}, f32[16,128,128]{1,2,0:T(8,128)S(1)}) fusion(f32[16,128,128]{1,2,0:T(8,128)S(1)} %get-tuple-element.413, f32[16,128]{1,0:T(8,128)S(1)} %broadcast_multiply_fusion, f32[16,128]{1,0:T(8,128)S(1)} %fusion.40, f32[2,8,128,128]{2,3,1,0:T(8,128)} %copy-done.4, f32[16,128]{1,0:T(8,128)S(1)} %add_rsqrt_fusion, ...), kind=kLoop, calls=%fused_computation.63 | loop fusion | flops 2881536 | bytes 3702848 | tf_op jit(solution)/shard_map/reduce_sum | solution.py:203
  88.9 2.8 %convolution_convert_fusion = bf16[16,64,128]{2,1,0:T(8,128)(2,1)} fusion(f32[16,128,128]{1,2,0:T(8,128)S(1)} %get-tuple-element.397, f32[16,128,64]{1,2,0:T(8,128)S(1)} %bitcast.116, f32[16,128]{1,0:T(8,128)S(1)} %get-tuple-element.411), kind=kOutput, calls=%fused_computation.52 | convolution fusion | flops 201588736 | bytes 1843200 | tf_op jit(solution)/shard_map/htn,htp->hnp/dot_general | solution.py:204
  91.8 3.3 %fusion.28 = (f32[16,128]{1,0:T(8,128)S(1)}, f32[16,128,128]{1,2,0:T(8,128)}) fusion(bf16[16,128,128]{1,2,0:T(8,128)(2,1)S(1)} %copy.121, f32[16,128,128]{2,1,0:T(8,128)} %copy-done.1, f32[16,128,128]{1,2,0:T(8,128)S(1)} %get-tuple-element.397), kind=kOutput, calls=%fused_computation.55 | convolution fusion | flops 403437568 | bytes 3678208 | tf_op jit(solution)/shard_map/hts,htp->hsp/dot_general | solution.py:195
  95.5 12.4 %all-reduce.1 = bf16[64]{0:T(256)(128)(2,1)S(1)} all-reduce(bf16[64]{0:T(256)(128)(2,1)S(1)} %dynamic-update-slice.1), channel_id=5, replica_groups=mesh['groups'=2,'seq'=4,'head'=2,'sub'=2] {'seq'}, use_global_device_ids=true, to_apply=%add.1 | all-reduce | flops 64 | bytes 256
  108.0 2.1 %convolution_multiply_fusion.3 = f32[16,128,64]{1,2,0:T(8,128)S(1)} fusion(f32[16,128,128]{1,2,0:T(8,128)S(1)} %get-tuple-element.397, f32[16,128]{1,0:T(8,128)S(1)} %get-tuple-element.411, f32[16,64,128]{2,1,0:T(8,128)S(1)} %get-tuple-element.293, f32[16,64,128]{2,1,0:T(8,128)} %param.19, f32[16]{0:T(128)S(1)} %get-tuple-element.294), kind=kOutput, calls=%fused_computation.47 | convolution fusion | flops 201719808 | bytes 2629696 | tf_op jit(solution)/shard_map/hnp,htp->htn/dot_general | solution.py:200
  112.4 2.9 %convolution_add_fusion.2 = f32[16,128,64]{1,2,0:T(8,128)} fusion(f32[16,128,64]{1,2,0:T(8,128)S(1)} %convolution_multiply_fusion.3, f32[16,128,128]{2,1,0:T(8,128)S(1)} %convolution_multiply_fusion.1, f32[16,128,64]{1,2,0:T(8,128)S(1)} %bitcast.119), kind=kOutput, calls=%fused_computation.48 | convolution fusion | flops 201457664 | bytes 2621440 | tf_op jit(solution)/shard_map/hts,hsn->htn/dot_general | solution.py:199
  115.3 6.2 %all-gather.9.cloned.1.call-done = bf16[64,64,128]{2,1,0:T(8,128)(2,1)} async-done(((bf16[16,64,128]{2,1,0:T(8,128)(2,1)}), bf16[64,64,128]{2,1,0:T(8,128)(2,1)}) %all-gather.9.cloned.1.call-update) | async-done | bytes 1048592 | tf_op jit(solution)/shard_map/all_gather | solution.py:48
  121.6 4.4 %while.48 = (s32[]{:T(128)}, f32[16,64,128]{2,1,0:T(8,128)S(1)}, f32[16]{0:T(128)S(1)}, s32[]{:T(128)}, bf16[4,16]{1,0:T(4,128)(2,1)S(1)}, /*index=5*/bf16[4,16,...) while((s32[]{:T(128)}, f32[16,64,128]{2,1,0:T(8,128)S(1)}, ...), condition=%wide.region_15.16_spmd, body=%wide.region_13.15_spmd.sunk | while | flops 786486 | bytes 1573487 | solution.py:65
  121.6 1.3 fusion.83
  123.0 1.3 fusion.83
  127.3 2.8 %fusion.29 = (f32[16,128]{1,0:T(8,128)S(1)}, bf16[16,128,128]{1,2,0:T(8,128)(2,1)}) fusion(bf16[16,128,128]{1,2,0:T(8,128)(2,1)S(1)} %copy.121, f32[16,128,128]{1,2,0:T(8,128)S(1)} %get-tuple-element.397, f32[16]{0:T(128)S(1)} %copy-done.15, f32[16,128,128]{1,2,0:T(8,128)S(1)} %copy-done.8, f32[16,64,128]{2,1,0:T(8,128)S(1)} %get-tuple-element.297, ...), kind=kOutput, calls=%fused_computation.56 | convolution fusion | flops 203290624 | bytes 4210752 | tf_op jit(solution)/shard_map/hsn,hnp->hsp/dot_general | solution.py:217
  (137 shorter events, 30.1 us)
Async XLA Ops:
  7.2 74.9 %all-gather.7.cloned.1.call-start = ((), (), s32[]{:S(2)}) async-start(), calls=%async_computation.1 | async-start | bytes 1310720 | tf_op jit(solution)/shard_map/all_gather | solution.py:26
  7.3 8.2 %copy-start.14 = (f32[16,128]{1,0:T(8,128)S(1)}, f32[16,128]{1,0:T(8,128)}, u32[]{:S(2)}) copy-start(f32[16,128]{1,0:T(8,128)} %param.17) | copy-start | bytes 24580
  7.3 8.8 %copy-start.12 = (bf16[2,128,128]{2,1,0:T(8,128)(2,1)S(1)}, bf16[2,128,128]{2,1,0:T(8,128)(2,1)}, u32[]{:S(2)}) copy-start(bf16[2,128,128]{2,1,0:T(8,128)(2,1)} %param.16) | copy-start | bytes 196612
  8.5 8.7 %copy-start = (bf16[16,128,128]{2,1,0:T(8,128)(2,1)S(1)}, bf16[16,128,128]{2,1,0:T(8,128)(2,1)}, u32[]{:S(2)}) copy-start(bf16[16,128,128]{2,1,0:T(8,128)(2,1)} %param.15) | copy-start | bytes 1572868
  8.5 34.5 %collective-permute-start = (bf16[2,2,128,128]{3,2,1,0:T(8,128)(2,1)S(1)}, bf16[2,2,128,128]{3,2,1,0:T(8,128)(2,1)S(1)}, u32[]{:S(2)}, u32[]{:S(2)}) collective-permute-start(bf16[2,2,128,128]{3,2,1,0:T(8,128)(2,1)S(1)} %get-tuple-element.406), channel_id=1, source_target_pairs={{0,4},{4,8},{8,12},{12,0},{1,5},{5,9},{9,13},{13,1},{2,6},{6,10},{... | collective-permute-start | bytes 393224 | tf_op jit(solution)/shard_map/ppermute | solution.py:141
  11.5 31.4 %collective-permute-start.1 = (bf16[2,2,128,128]{3,2,1,0:T(8,128)(2,1)S(1)}, bf16[2,2,128,128]{3,2,1,0:T(8,128)(2,1)S(1)}, u32[]{:S(2)}, u32[]{:S(2)}) collective-permute-start(bf16[2,2,128,128]{3,2,1,0:T(8,128)(2,1)S(1)} %get-tuple-element.405), channel_id=1, source_target_pairs={{0,8},{4,12},{8,0},{12,4},{1,9},{5,13},{9,1},{13,5},{2,10},{6,14},... | collective-permute-start | bytes 393224 | tf_op jit(solution)/shard_map/ppermute | solution.py:141
  14.1 28.9 %collective-permute-start.2 = (bf16[2,2,128,128]{3,2,1,0:T(8,128)(2,1)S(1)}, bf16[2,2,128,128]{3,2,1,0:T(8,128)(2,1)S(1)}, u32[]{:S(2)}, u32[]{:S(2)}) collective-permute-start(bf16[2,2,128,128]{3,2,1,0:T(8,128)(2,1)S(1)} %get-tuple-element.407), channel_id=1, source_target_pairs={{0,12},{4,0},{8,4},{12,8},{1,13},{5,1},{9,5},{13,9},{2,14},{6,2},{... | collective-permute-start | bytes 393224 | tf_op jit(solution)/shard_map/ppermute | solution.py:141
  16.3 0.8 copy-start.5
  18.4 0.9 copy-start.13
  58.8 23.1 %all-to-all-start = ((bf16[2,8,128,128]{2,3,0,1:T(8,128)(2,1)}), bf16[2,8,128,128]{2,3,0,1:T(8,128)(2,1)S(1)}, u32[]{:S(2)}, u32[]{:S(2)}) async-start(bf16[2,8,128,128]{2,3,0,1:T(8,128)(2,1)} %copy.127), calls=%async_computation | async-start | bytes 1048576 | tf_op jit(solution)/shard_map/all_to_all | solution.py:151
  63.0 58.5 %all-gather.9.cloned.1.call-start = ((), (), s32[]{:S(2)}) async-start(), calls=%async_computation.2 | async-start | bytes 1310720 | tf_op jit(solution)/shard_map/all_gather | solution.py:48
  63.3 0.7 copy-start.16
  78.6 1.0 copy-start.1
  81.9 4.8 %copy-start.4 = (f32[2,8,128,128]{2,3,1,0:T(8,128)}, f32[2,8,128,128]{2,3,1,0:T(8,128)S(1)}, u32[]{:S(2)}) copy-start(f32[2,8,128,128]{2,3,1,0:T(8,128)S(1)} %copy.128) | copy-start | bytes 3145732
  82.4 1.0 copy-start.11
  82.4 1.0 copy-start.15
  110.1 2.3 %copy-start.6 = (f32[2,8,128,64]{2,3,1,0:T(8,128)S(1)}, f32[2,8,128,64]{2,3,1,0:T(8,128)}, u32[]{:S(2)}) copy-start(f32[2,8,128,64]{2,3,1,0:T(8,128)} %copy-done.5) | copy-start | bytes 1572868
  111.3 1.0 copy-start.2
  126.0 1.2 copy-start.8
  126.0 1.3 copy-start.7
  127.3 2.8 %copy-start.3 = (f32[16,128,128]{2,1,0:T(8,128)S(1)}, f32[16,128,128]{2,1,0:T(8,128)}, u32[]{:S(2)}) copy-start(f32[16,128,128]{2,1,0:T(8,128)} %copy-done.2) | copy-start | bytes 3145732
  130.1 1.0 copy-start.9
  131.2 1.0 copy-start.10
Sparse Core Ops, SparseCore 0:
  18.5 32.5 all-gather.6
  91.9 29.5 all-gather.8
